TPU v7x, 512 devices: a whole 4x8x8 slice. The times are simulated.
512 devices in a mesh: sub: 8 (over x, core), seq: 8 (over y), exp: 8 (over z).
Axes of the slice: x: 4, y: 8, z: 8, core: 2. Of those that a mesh axis runs over, the one named last changes fastest.
Arguments:
- node_features: bfloat16 [64, 1536, 1024], P(('sub', 'exp'), 'seq'), parts along dimension 0, may hold values from -24 to 24
- block_mask: int32 [64, 12, 12], P(('sub', 'exp')), parts along dimension 0, may hold values from 0 to 1, as said below
- w_qkv: bfloat16 [1024, 3072], P('exp', 'seq'), may hold values from -4 to 4
- w_out: bfloat16 [1024, 1024], P('seq', 'exp'), may hold values from -0.1875 to 0.1875
- norm_gain: float32 [1024], replicated, may hold values from 0.5 to 1.5
- routes: int32 [64, 1536, 2], P(('sub', 'exp'), 'seq'), parts along dimension 0, may hold values from 0 to 63, all different within a row; in each aligned block of 192 rows (0 to 191, 192 to 383, ..., all dimensions but the last counted through in order) at most 12 rows name the same one
- gates: float32 [64, 1536, 2], P(('sub', 'exp'), 'seq'), parts along dimension 0, may hold values from 0.1 to 1
- w_gate_up: bfloat16 [64, 1024, 1024], P(('seq', 'exp')), may hold values from -0.1875 to 0.1875
- w_down: bfloat16 [64, 512, 1024], P(('seq', 'exp')), may hold values from -0.25 to 0.25
Outputs:
- layer_out: bfloat16 [64, 1536, 1024], P(('sub', 'exp'), 'seq'), parts along dimension 0
There are 8 independent parts, one for each index of `sub`. A program takes and returns all parts, laid end to end along the dimension named above; an argument that names none is the same for every part. Nothing has to cross between parts.
Inputs may be any that keep to these rules, and one draw needn't show every extreme that they name: In each aligned block of 192 rows (one device's nodes, subgraphs then nodes in order) no expert is named by more than 12 of the rows' routes, a bound that some block reaches; the 2 experts of a node differ. `block_mask`: the diagonal blocks are 1.
All inputs are finite; a program needn't handle non-finite values.
Results may differ from a plain program's by a relative error of at most 0.0065.
The roundings to bfloat16 on the way count: a program that leaves them out, or rounds other values in their place, can miss the bound.
Values may be sent and summed in bfloat16 or wider, within the bound.
No kernel may reach another device: no remote copies, remote signals or barrier semaphores. Data moves between devices by JAX's collectives and lax.ppermute only.
A program may use at most 64 MiB of HBM per device.

v0:
```python
import math
import jax
import jax.numpy as jnp
from jax import lax
from jax.sharding import PartitionSpec as P

HEAD_DIM = 64
TOP = 2
BLOCK = 128


def per_device(
    node_features, block_mask, w_qkv, w_out, norm_gain, routes, gates, w_gate_up, w_down
):
    feats = node_features[0]
    node_dev, width = feats.shape
    seq_count = lax.axis_size("seq")
    exp_count = lax.axis_size("exp")
    experts = seq_count * exp_count * w_gate_up.shape[0]
    head_cols = w_qkv.shape[1]
    qkv_all, out_all = (
        lax.all_gather(w_qkv[None], ("seq", "exp"), axis=0, tiled=True),
        lax.all_gather(w_out[None], ("seq", "exp"), axis=0, tiled=True),
    )
    qkv_tiles = qkv_all.reshape(seq_count, exp_count, w_qkv.shape[0], head_cols)
    local_proj = jnp.einsum(
        "nek,sekc->nsc",
        feats.reshape(node_dev, exp_count, w_qkv.shape[0]),
        qkv_tiles,
        preferred_element_type=jnp.float32,
    )
    local_proj = local_proj.astype(jnp.bfloat16).reshape(node_dev, seq_count * head_cols)
    projected = lax.all_to_all(local_proj, "seq", split_axis=1, concat_axis=0, tiled=True)
    nodes = projected.shape[0]
    heads_here = head_cols // (3 * HEAD_DIM)
    split = projected.reshape(nodes, heads_here, 3, HEAD_DIM)
    query = split[:, :, 0]
    keys = split[:, :, 1]
    values = split[:, :, 2]
    col_mask = jnp.repeat(block_mask[0], BLOCK, axis=1) > 0
    span = math.gcd(nodes, 512)
    scale = 1.0 / math.sqrt(HEAD_DIM)

    def attend(index):
        start = index * span
        rows_query = lax.dynamic_slice_in_dim(query, start, span, 0)
        rows_mask = lax.dynamic_slice_in_dim(col_mask, start // BLOCK, span // BLOCK, 0)
        allowed = jnp.repeat(rows_mask, BLOCK, axis=0)
        scores = (
            jnp.einsum("qhd,khd->hqk", rows_query, keys, preferred_element_type=jnp.float32) * scale
        )
        scores = jnp.where(allowed[None], scores, -1e30)
        top = jnp.max(scores, axis=-1, keepdims=True)
        weights = jnp.exp(scores - top)
        probs = (weights / jnp.sum(weights, axis=-1, keepdims=True)).astype(jnp.bfloat16)
        return jnp.einsum("hqk,khd->qhd", probs, values, preferred_element_type=jnp.float32).astype(
            jnp.bfloat16
        )

    blocks = lax.map(attend, jnp.arange(nodes // span, dtype=jnp.int32))
    attended = blocks.reshape(nodes, heads_here * HEAD_DIM)
    node_attended = lax.all_to_all(attended, "seq", split_axis=0, concat_axis=1, tiled=True)
    out_tiles = out_all.reshape(seq_count, exp_count, w_out.shape[0], w_out.shape[1])
    attn_out = jnp.einsum(
        "nsk,sekc->nec",
        node_attended.reshape(node_dev, seq_count, w_out.shape[0]),
        out_tiles,
        preferred_element_type=jnp.float32,
    )
    mixed = feats.astype(jnp.float32) + attn_out.reshape(node_dev, width)
    mean_square = jnp.mean(mixed * mixed, axis=-1, keepdims=True)
    normed = (mixed * lax.rsqrt(mean_square + 1e-06) * norm_gain).astype(jnp.bfloat16)
    capacity = 2 * TOP * node_dev // experts
    pair_routes = routes[0].reshape(node_dev * TOP)
    onehot = (pair_routes[:, None] == jnp.arange(experts, dtype=jnp.int32)).astype(jnp.int32)
    earlier = jnp.cumsum(onehot, axis=0, dtype=jnp.int32) - onehot
    slots = jnp.sum(earlier * onehot, axis=1, dtype=jnp.int32)
    position = pair_routes * capacity + slots
    outgoing = (
        jnp.zeros((experts * capacity, width), jnp.bfloat16)
        .at[position]
        .set(jnp.repeat(normed, TOP, axis=0))
    )
    outgoing = outgoing.reshape(experts, capacity, width)
    hidden_units = w_down.shape[1]
    received = lax.all_to_all(outgoing, ("seq", "exp"), split_axis=0, concat_axis=0, tiled=True)
    sources, items, columns = received.shape
    flat_rows = received.reshape(sources * items, columns)
    both = jnp.dot(flat_rows, w_gate_up[0], preferred_element_type=jnp.float32)
    hidden = (jax.nn.silu(both[:, :hidden_units]) * both[:, hidden_units:]).astype(jnp.bfloat16)
    result = jnp.dot(hidden, w_down[0], preferred_element_type=jnp.float32).astype(jnp.bfloat16)
    processed = result.reshape(sources, items, columns)
    returned = lax.all_to_all(
        processed, ("seq", "exp"), split_axis=0, concat_axis=0, tiled=True
    ).reshape(experts * capacity, width)
    picked = returned[position].astype(jnp.float32).reshape(node_dev, TOP, width)
    expert_sum = jnp.sum(picked * gates[0][:, :, None], axis=1)
    return (mixed + expert_sum).astype(jnp.bfloat16)[None]


def solution(mesh):
    in_specs = (
        P(("sub", "exp"), "seq", None),
        P(("sub", "exp"), None, None),
        P("exp", "seq"),
        P("seq", "exp"),
        P(),
        P(("sub", "exp"), "seq", None),
        P(("sub", "exp"), "seq", None),
        P(("seq", "exp"), None, None),
        P(("seq", "exp"), None, None),
    )
    out_specs = P(("sub", "exp"), "seq", None)
    return jax.shard_map(
        per_device, mesh=mesh, in_specs=in_specs, out_specs=out_specs, check_vma=False
    )
```

profile of v0, /device:TPU:24, one launch (start us, length us, event | category | flops | bytes accessed | tf_op | source)
XLA Modules:
  0.0 382.8 jit_solution(14159090257780799350)
XLA Ops:
  6.5 0.7 all-gather.5.cloned.1.call-update
  7.3 1.1 copy.33
  8.3 97.1 %all-gather.5.cloned.1.call-done = bf16[8192,384]{1,0:T(8,128)(2,1)} async-done(((bf16[128,384]{1,0:T(8,128)(2,1)}), bf16[8192,384]{1,0:T(8,128)(2,1)}) %all-gather.5.cloned.1.call-update) | async-done | bytes 6291472 | tf_op jit(solution)/shard_map/all_gather | solution.py:22
  105.4 5.2 %bitcast_convert_fusion = bf16[192,8,384]{2,0,1:T(8,128)(2,1)} fusion(bf16[8,8,128,384]{3,2,1,0:T(8,128)(2,1)} %bitcast.99, bf16[192,8,128]{2,1,0:T(8,128)(2,1)S(1)} %bitcast.103), kind=kOutput, calls=%fused_computation.28 | convolution fusion | flops 1208549376 | bytes 7864320 | tf_op jit(solution)/shard_map/nek,sekc->nsc/dot_general | solution.py:26
  110.7 6.1 %all-to-all-start = ((bf16[192,8,384]{2,0,1:T(8,128)(2,1)}), bf16[192,8,384]{2,0,1:T(8,128)(2,1)S(1)}, u32[]{:S(2)}, u32[]{:S(2)}) async-start(bf16[192,8,384]{2,0,1:T(8,128)(2,1)} %bitcast_convert_fusion), calls=%async_computation | async-start | bytes 2359296 | tf_op jit(solution)/shard_map/all_to_all | solution.py:33
  116.7 0.7 all-gather.7.cloned.1.call-update
  118.1 26.0 %all-to-all-done = bf16[192,8,384]{2,0,1:T(8,128)(2,1)S(1)} async-done(((bf16[192,8,384]{2,0,1:T(8,128)(2,1)}), bf16[192,8,384]{2,0,1:T(8,128)(2,1)S(1)}, u32[]{:S(2)}, u32[]{:S(2)}) %all-to-all-start) | async-done | bytes 1179680 | tf_op jit(solution)/shard_map/all_to_all | solution.py:33
  144.1 2.0 copy.18
  146.1 2.9 reshape.112
  149.0 1.1 slice_bitcast_fusion
  150.1 28.0 %while.12 = (s32[]{:T(128)}, bf16[3,512,2,64]{1,3,2,0:T(8,128)(2,1)}, s32[3]{0:T(128)S(1)}, pred[12,1536]{1,0:T(8,128)(4,1)S(1)}, bf16[1536,2,64]{0,2,1:T(8,128)...) while((s32[]{:T(128)}, ...), condition=%wide.region_3.4_spmd, body=%wide.region_0.3_spmd.sunk | while | flops 618205184 | bytes 5532574 | solution.py:60
  150.1 0.6 dynamic_slice.40
  151.3 0.2 broadcast_in_dim.104
  151.5 3.5 fusion.73
  155.0 4.4 %fusion.74 = bf16[3,512,2,64]{1,3,2,0:T(8,128)(2,1)} fusion(bf16[3,512,2,64]{1,3,2,0:T(8,128)(2,1)} %get-tuple-element.174, s32[]{:T(128)} %get-tuple-element.173, bf16[1536,2,64]{0,2,1:T(8,128)(2,1)S(1)} %copy-done.3, f32[2,512]{1,0:T(2,128)S(1)} %fusion.73, pred[512,1536]{1,0:T(8,128)(4,1)S(1)} %bitcast.97, ...), kind=kOutput, calls=%fused_computation.13.clone.1 | convolution fusion | flops 410585600 | bytes 1839620 | tf_op jit(solution)/shard_map/while/body/eval_jaxpr/hqk,khd->qhd/dot_general | solution.py:56
  159.4 0.6 dynamic_slice.40
  160.6 0.2 broadcast_in_dim.104
  160.9 3.5 fusion.73
  164.4 4.4 %fusion.74 = bf16[3,512,2,64]{1,3,2,0:T(8,128)(2,1)} fusion(bf16[3,512,2,64]{1,3,2,0:T(8,128)(2,1)} %get-tuple-element.174, s32[]{:T(128)} %get-tuple-element.173, bf16[1536,2,64]{0,2,1:T(8,128)(2,1)S(1)} %copy-done.3, f32[2,512]{1,0:T(2,128)S(1)} %fusion.73, pred[512,1536]{1,0:T(8,128)(4,1)S(1)} %bitcast.97, ...), kind=kOutput, calls=%fused_computation.13.clone.1 | convolution fusion | flops 410585600 | bytes 1839620 | tf_op jit(solution)/shard_map/while/body/eval_jaxpr/hqk,khd->qhd/dot_general | solution.py:56
  168.8 0.6 dynamic_slice.40
  170.0 0.2 broadcast_in_dim.104
  170.2 3.5 fusion.73
  173.7 4.4 %fusion.74 = bf16[3,512,2,64]{1,3,2,0:T(8,128)(2,1)} fusion(bf16[3,512,2,64]{1,3,2,0:T(8,128)(2,1)} %get-tuple-element.174, s32[]{:T(128)} %get-tuple-element.173, bf16[1536,2,64]{0,2,1:T(8,128)(2,1)S(1)} %copy-done.3, f32[2,512]{1,0:T(2,128)S(1)} %fusion.73, pred[512,1536]{1,0:T(8,128)(4,1)S(1)} %bitcast.97, ...), kind=kOutput, calls=%fused_computation.13.clone.1 | convolution fusion | flops 410585600 | bytes 1839620 | tf_op jit(solution)/shard_map/while/body/eval_jaxpr/hqk,khd->qhd/dot_general | solution.py:56
  178.1 2.2 copy.28
  180.3 1.1 reshape.145
  181.4 8.0 %all-to-all-start.1 = ((bf16[8,192,128]{2,1,0:T(8,128)(2,1)}), bf16[8,192,128]{2,1,0:T(8,128)(2,1)S(1)}, u32[]{:S(2)}, u32[]{:S(2)}) async-start(bf16[8,192,128]{2,1,0:T(8,128)(2,1)} %reshape.145), calls=%async_computation.1 | async-start | bytes 786432 | tf_op jit(solution)/shard_map/all_to_all | solution.py:62
  189.4 0.9 reduce-window.6
  190.3 0.2 slice_reduce_fusion
  191.0 16.6 %all-gather.7.cloned.1.call-done = bf16[8192,128]{1,0:T(8,128)(2,1)} async-done(((bf16[128,128]{1,0:T(8,128)(2,1)}), bf16[8192,128]{1,0:T(8,128)(2,1)}) %all-gather.7.cloned.1.call-update) | async-done | bytes 2097168 | tf_op jit(solution)/shard_map/all_gather | solution.py:23
  207.6 4.0 %copy.21 = bf16[8,8,128,128]{2,3,1,0:T(8,128)(2,1)} copy(bf16[8,8,128,128]{3,2,1,0:T(8,128)(2,1)} %bitcast.101) | data formatting | bytes 4194304 | tf_op jit(solution)/shard_map/reshape | solution.py:63
  211.6 0.7 copy-done.2
  212.3 2.7 multiply_reduce_fusion.1
  215.2 1.3 broadcast_in_dim.69
  216.5 3.0 reshape.134
  219.4 4.0 %scatter_custom_fusion = bf16[768,1024]{1,0:T(8,128)(2,1)} fusion(s32[384]{0:T(512)S(1)} %fusion.50, bf16[384,1024]{1,0:T(8,128)(2,1)} %reshape.134, bf16[]{:T(256)} %constant.96.clone.1), kind=kCustom, calls=%fused_computation.42 | custom fusion | bytes 1573376 | tf_op jit(solution)/shard_map/scatter | solution.py:82
  223.4 3.6 reshape.116
  227.0 59.8 %all_to_all.39 = bf16[64,12,1024]{2,1,0:T(8,128)(2,1)} all-to-all(bf16[64,12,1024]{2,1,0:T(8,128)(2,1)} %reshape.116), channel_id=1, replica_groups=mesh['sub'=8,'seq'=8,'exp'=8] {'seq','exp'}, dimensions={0} | all-to-all | bytes 3145728 | tf_op jit(solution)/shard_map/all_to_all | solution.py:86
  286.8 3.6 reshape.117
  290.4 3.3 fusion.33
  293.7 2.2 convolution_convert_fusion
  295.9 3.6 reshape.118
  299.5 7.7 %all-to-all-start.3 = ((bf16[64,12,1024]{2,1,0:T(8,128)(2,1)}), bf16[64,12,1024]{2,1,0:T(8,128)(2,1)}, u32[]{:S(2)}, u32[]{:S(2)}) async-start(bf16[64,12,1024]{2,1,0:T(8,128)(2,1)} %reshape.118), calls=%async_computation.3 | async-start | bytes 4194304 | tf_op jit(solution)/shard_map/all_to_all | solution.py:93
  307.3 52.9 %all-to-all-done.3 = bf16[64,12,1024]{2,1,0:T(8,128)(2,1)} async-done(((bf16[64,12,1024]{2,1,0:T(8,128)(2,1)}), bf16[64,12,1024]{2,1,0:T(8,128)(2,1)}, u32[]{:S(2)}, u32[]{:S(2)}) %all-to-all-start.3) | async-done | bytes 1572896 | tf_op jit(solution)/shard_map/all_to_all | solution.py:93
  360.2 3.6 reshape.119
  363.8 5.0 %gather_fusion = bf16[384,1024]{1,0:T(8,128)(2,1)} fusion(bf16[768,1024]{1,0:T(8,128)(2,1)} %reshape.119, s32[1024]{0:T(1024)S(1)} %pad_clamp_fusion), kind=kCustom, calls=%fused_computation | custom fusion | bytes 1574400 | tf_op jit(solution)/shard_map/gather | solution.py:96
  368.7 3.0 reshape.121
  371.7 3.4 multiply_reduce_fusion
  375.1 0.8 fusion.42
  (48 shorter events, 1.4 us)
Async XLA Ops:
  6.5 283.9 %copy-start = (bf16[1,1024,1024]{2,1,0:T(8,128)(2,1)S(1)}, bf16[1,1024,1024]{2,1,0:T(8,128)(2,1)}, u32[]{:S(2)}) copy-start(bf16[1,1024,1024]{2,1,0:T(8,128)(2,1)} %param.18) | copy-start | bytes 6291460
  6.5 98.9 %all-gather.5.cloned.1.call-start = ((), (), s32[]{:S(2)}) async-start(), calls=%async_computation.4 | async-start | bytes 6389760 | tf_op jit(solution)/shard_map/all_gather | solution.py:22
  110.7 6.8 %copy-start.4 = (s32[1,192,2]{1,2,0:T(2,128)S(1)}, s32[1,192,2]{1,2,0:T(2,128)}, u32[]{:S(2)}) copy-start(s32[1,192,2]{1,2,0:T(2,128)} %param.16) | copy-start | bytes 4612
  110.7 7.2 %copy-start.5 = (s32[1,12,12]{2,0,1:T(1,128)S(1)}, s32[1,12,12]{2,0,1:T(1,128)}, u32[]{:S(2)}) copy-start(s32[1,12,12]{2,0,1:T(1,128)} %param.12) | copy-start | bytes 1732
  110.7 33.4 %all-to-all-start = ((bf16[192,8,384]{2,0,1:T(8,128)(2,1)}), bf16[192,8,384]{2,0,1:T(8,128)(2,1)S(1)}, u32[]{:S(2)}, u32[]{:S(2)}) async-start(bf16[192,8,384]{2,0,1:T(8,128)(2,1)} %bitcast_convert_fusion), calls=%async_computation | async-start | bytes 2359296 | tf_op jit(solution)/shard_map/all_to_all | solution.py:33
  116.7 90.9 %all-gather.7.cloned.1.call-start = ((), (), s32[]{:S(2)}) async-start(), calls=%async_computation.5 | async-start | bytes 2129920 | tf_op jit(solution)/shard_map/all_gather | solution.py:23
  151.5 3.5 copy-start.3
  160.9 3.5 copy-start.3
  170.2 3.5 copy-start.3
  181.4 30.2 %all-to-all-start.1 = ((bf16[8,192,128]{2,1,0:T(8,128)(2,1)}), bf16[8,192,128]{2,1,0:T(8,128)(2,1)S(1)}, u32[]{:S(2)}, u32[]{:S(2)}) async-start(bf16[8,192,128]{2,1,0:T(8,128)(2,1)} %reshape.145), calls=%async_computation.1 | async-start | bytes 786432 | tf_op jit(solution)/shard_map/all_to_all | solution.py:62
  207.6 4.7 %copy-start.1 = (bf16[1,192,1024]{2,1,0:T(8,128)(2,1)S(1)}, bf16[1,192,1024]{2,1,0:T(8,128)(2,1)}, u32[]{:S(2)}) copy-start(bf16[1,192,1024]{2,1,0:T(8,128)(2,1)} %param.11) | copy-start | bytes 1179652
  211.6 3.4 copy-start.6
  211.6 0.7 copy-start.2
  290.4 3.3 copy-start.8
  299.5 7.7 %copy-start.7 = (f32[1,192,2]{1,2,0:T(2,128)S(1)}, f32[1,192,2]{1,2,0:T(2,128)}, u32[]{:S(2)}) copy-start(f32[1,192,2]{1,2,0:T(2,128)} %param.17) | copy-start | bytes 4612
  299.5 60.7 %all-to-all-start.3 = ((bf16[64,12,1024]{2,1,0:T(8,128)(2,1)}), bf16[64,12,1024]{2,1,0:T(8,128)(2,1)}, u32[]{:S(2)}, u32[]{:S(2)}) async-start(bf16[64,12,1024]{2,1,0:T(8,128)(2,1)} %reshape.118), calls=%async_computation.3 | async-start | bytes 4194304 | tf_op jit(solution)/shard_map/all_to_all | solution.py:93
Sparse Core Ops, SparseCore 0:
  10.4 94.9 all-gather.4
  120.6 86.9 all-gather.6
where the time goes:
time: 384 us; the launch traced here: 383 us
  waiting for transfers between devices  194 us (51%)
  blocking collectives  59.8 us (16%)
  local copies, waits for them, and re-layouts  49.3 us (13%)
  matrix products  37 us (10%)
  starting transfers between devices  21.8 us (6%)
  between operations  13.6 us (4%)
  other arithmetic  5.53 us (1%)
    all_gather x1, waiting for transfers between devices, per_device(): lax.all_gather(w_qkv[None], ('seq', 'exp'), axis=0, tiled=True)  97.1 us
    all_to_all x1, blocking collectives, per_device(): lax.all_to_all(outgoing, ('seq', 'exp'), split_axis=0, concat_axis=0, til...  59.8 us
    all_to_all x1, waiting for transfers between devices, per_device(): lax.all_to_all(processed, ('seq', 'exp'), split_axis=0, concat_axis=0, ti...  52.9 us
    all_to_all x1, waiting for transfers between devices, per_device(): lax.all_to_all(local_proj, 'seq', split_axis=1, concat_axis=0, tiled=True)  26 us
    all_gather x1, waiting for transfers between devices, per_device(): lax.all_gather(w_out[None], ('seq', 'exp'), axis=0, tiled=True)  16.6 us
    dot_general x3, matrix products, attend(): jnp.einsum('hqk,khd->qhd', probs, values, preferred_element_type=jnp.floa...  13.2 us
    sub x3, matrix products, attend(): weights = jnp.exp(scores - top)  10.4 us
    all_to_all x1, starting transfers between devices, per_device(): lax.all_to_all(attended, 'seq', split_axis=0, concat_axis=1, tiled=True)  8.03 us
  transfers between devices with their start and end apart: 5, of which 4 were waited for; matrix products, arithmetic and copies ran while one was open for 11% of the time, Pallas kernels for 0%

commit v1 on v0

--- a/solution.py
+++ b/solution.py
@@ -7,6 +7,12 @@
 HEAD_DIM = 64
 TOP = 2
 BLOCK = 128
+
+
+def gather_by_exchange(x, axis, dim):
+    devices = lax.axis_size(axis)
+    repeats = [devices if d == dim else 1 for d in range(x.ndim)]
+    return lax.all_to_all(jnp.tile(x, repeats), axis, split_axis=dim, concat_axis=dim, tiled=True)
 
 
 def per_device(
@@ -19,7 +25,7 @@
     experts = seq_count * exp_count * w_gate_up.shape[0]
     head_cols = w_qkv.shape[1]
     qkv_all, out_all = (
-        lax.all_gather(w_qkv[None], ("seq", "exp"), axis=0, tiled=True),
+        gather_by_exchange(w_qkv[None], ("seq", "exp"), 0),
         lax.all_gather(w_out[None], ("seq", "exp"), axis=0, tiled=True),
     )
     qkv_tiles = qkv_all.reshape(seq_count, exp_count, w_qkv.shape[0], head_cols)

time: 384 us -> 539 us (1.40)
  the two profiles are of different devices: /device:TPU:24 before, /device:TPU:30 now
where the time goes in v1:
time: 539 us; the launch traced here: 537 us
  waiting for transfers between devices  306 us (57%)
  blocking collectives  61.3 us (11%)
  starting transfers between devices  59.1 us (11%)
  local copies, waits for them, and re-layouts  53 us (10%)
  matrix products  37 us (7%)
  between operations  13.6 us (3%)
  other arithmetic  5.53 us (1%)
    all_to_all x1, waiting for transfers between devices, gather_by_exchange(): lax.all_to_all(jnp.tile(x, repeats), axis, split_axis=dim, concat_axis=di...  202 us
    all_to_all x1, blocking collectives, per_device(): lax.all_to_all(outgoing, ('seq', 'exp'), split_axis=0, concat_axis=0, til...  61.3 us
    all_to_all x1, waiting for transfers between devices, per_device(): lax.all_to_all(processed, ('seq', 'exp'), split_axis=0, concat_axis=0, ti...  51.5 us
    all_to_all x1, starting transfers between devices, per_device(): lax.all_to_all(local_proj, 'seq', split_axis=1, concat_axis=0, tiled=True)  26.6 us
    all_gather x1, waiting for transfers between devices, per_device(): lax.all_gather(w_out[None], ('seq', 'exp'), axis=0, tiled=True)  26.6 us
    all_to_all x1, waiting for transfers between devices, per_device(): lax.all_to_all(local_proj, 'seq', split_axis=1, concat_axis=0, tiled=True)  24.6 us
    all_to_all x1, starting transfers between devices, gather_by_exchange(): lax.all_to_all(jnp.tile(x, repeats), axis, split_axis=dim, concat_axis=di...  16.7 us
    dot_general x3, matrix products, attend(): jnp.einsum('hqk,khd->qhd', probs, values, preferred_element_type=jnp.floa...  13.2 us
  transfers between devices with their start and end apart: 5, of which 4 were waited for; matrix products, arithmetic and copies ran while one was open for 8% of the time, Pallas kernels for 0%

profile of v1, /device:TPU:30, one launch (start us, length us, event | category | flops | bytes accessed | tf_op | source)
XLA Modules:
  0.0 537.1 jit_solution(10195134929377699106)
XLA Ops:
  6.5 4.7 tile.2
  11.2 16.7 %all-to-all-start = ((bf16[64,128,384]{2,1,0:T(8,128)(2,1)}), bf16[64,128,384]{2,1,0:T(8,128)(2,1)}, u32[]{:S(2)}, u32[]{:S(2)}) async-start(bf16[64,128,384]{2,1,0:T(8,128)(2,1)} %tile.2), calls=%async_computation | async-start | bytes 12582912 | tf_op jit(solution)/shard_map/all_to_all | solution.py:15
  28.0 202.4 %all-to-all-done = bf16[64,128,384]{2,1,0:T(8,128)(2,1)} async-done(((bf16[64,128,384]{2,1,0:T(8,128)(2,1)}), bf16[64,128,384]{2,1,0:T(8,128)(2,1)}, u32[]{:S(2)}, u32[]{:S(2)}) %all-to-all-start) | async-done | bytes 6291488 | tf_op jit(solution)/shard_map/all_to_all | solution.py:15
  230.5 5.2 bitcast_convert_fusion
  235.7 26.6 %all-to-all-start.1 = ((bf16[192,8,384]{2,0,1:T(8,128)(2,1)}), bf16[192,8,384]{2,0,1:T(8,128)(2,1)S(1)}, u32[]{:S(2)}, u32[]{:S(2)}) async-start(bf16[192,8,384]{2,0,1:T(8,128)(2,1)} %bitcast_convert_fusion), calls=%async_computation.1 | async-start | bytes 2359296 | tf_op jit(solution)/shard_map/all_to_all | solution.py:39
  262.3 0.7 all-gather.3.cloned.1.call-update
  263.7 24.6 %all-to-all-done.1 = bf16[192,8,384]{2,0,1:T(8,128)(2,1)S(1)} async-done(((bf16[192,8,384]{2,0,1:T(8,128)(2,1)}), bf16[192,8,384]{2,0,1:T(8,128)(2,1)S(1)}, u32[]{:S(2)}, u32[]{:S(2)}) %all-to-all-start.1) | async-done | bytes 1179680 | tf_op jit(solution)/shard_map/all_to_all | solution.py:39
  288.2 2.0 copy.18
  290.3 2.9 reshape.115
  293.2 1.1 slice_bitcast_fusion
  294.2 28.0 %while.12 = (s32[]{:T(128)}, bf16[3,512,2,64]{1,3,2,0:T(8,128)(2,1)}, s32[3]{0:T(128)S(1)}, pred[12,1536]{1,0:T(8,128)(4,1)S(1)}, bf16[1536,2,64]{0,2,1:T(8,128)...) while((s32[]{:T(128)}, ...), condition=%wide.region_3.4_spmd, body=%wide.region_0.3_spmd.sunk | while | flops 618205184 | bytes 5532574 | solution.py:66
  294.2 0.6 dynamic_slice.40
  295.4 0.2 broadcast_in_dim.100
  295.7 3.5 fusion.73
  299.1 4.4 fusion.74
  303.6 0.6 dynamic_slice.40
  304.8 0.2 broadcast_in_dim.100
  305.0 3.5 fusion.73
  308.5 4.4 fusion.74
  312.9 0.6 dynamic_slice.40
  314.1 0.2 broadcast_in_dim.100
  314.3 3.5 fusion.73
  317.8 4.4 fusion.74
  322.2 2.2 copy.28
  324.4 1.1 reshape.146
  325.5 6.7 %all-to-all-start.2 = ((bf16[8,192,128]{2,1,0:T(8,128)(2,1)}), bf16[8,192,128]{2,1,0:T(8,128)(2,1)S(1)}, u32[]{:S(2)}, u32[]{:S(2)}) async-start(bf16[8,192,128]{2,1,0:T(8,128)(2,1)} %reshape.146), calls=%async_computation.2 | async-start | bytes 786432 | tf_op jit(solution)/shard_map/all_to_all | solution.py:68
  332.2 0.9 reduce-window.6
  333.1 0.2 slice_reduce_fusion
  333.8 26.6 %all-gather.3.cloned.1.call-done = bf16[8192,128]{1,0:T(8,128)(2,1)} async-done(((bf16[128,128]{1,0:T(8,128)(2,1)}), bf16[8192,128]{1,0:T(8,128)(2,1)}) %all-gather.3.cloned.1.call-update) | async-done | bytes 2097168 | tf_op jit(solution)/shard_map/all_gather | solution.py:29
  360.4 4.0 copy.21
  364.4 0.7 copy-done.3
  365.1 2.7 multiply_reduce_fusion.1
  368.0 1.3 broadcast_in_dim.65
  369.3 3.0 reshape.137
  372.2 4.0 scatter_custom_fusion
  376.2 3.6 reshape.119
  379.8 61.3 %all_to_all.44 = bf16[64,12,1024]{2,1,0:T(8,128)(2,1)} all-to-all(bf16[64,12,1024]{2,1,0:T(8,128)(2,1)} %reshape.119), channel_id=1, replica_groups=mesh['sub'=8,'seq'=8,'exp'=8] {'seq','exp'}, dimensions={0} | all-to-all | bytes 3145728 | tf_op jit(solution)/shard_map/all_to_all | solution.py:92
  441.1 3.6 reshape.120
  444.7 3.3 fusion.33
  448.0 2.2 convolution_convert_fusion
  450.2 3.6 reshape.121
  453.8 9.1 %all-to-all-start.4 = ((bf16[64,12,1024]{2,1,0:T(8,128)(2,1)}), bf16[64,12,1024]{2,1,0:T(8,128)(2,1)}, u32[]{:S(2)}, u32[]{:S(2)}) async-start(bf16[64,12,1024]{2,1,0:T(8,128)(2,1)} %reshape.121), calls=%async_computation.4 | async-start | bytes 4194304 | tf_op jit(solution)/shard_map/all_to_all | solution.py:99
  463.0 51.5 %all-to-all-done.4 = bf16[64,12,1024]{2,1,0:T(8,128)(2,1)} async-done(((bf16[64,12,1024]{2,1,0:T(8,128)(2,1)}), bf16[64,12,1024]{2,1,0:T(8,128)(2,1)}, u32[]{:S(2)}, u32[]{:S(2)}) %all-to-all-start.4) | async-done | bytes 1572896 | tf_op jit(solution)/shard_map/all_to_all | solution.py:99
  514.5 3.6 reshape.122
  518.1 5.0 gather_fusion
  523.1 3.0 reshape.124
  526.0 3.4 multiply_reduce_fusion
  529.5 0.8 fusion.42
  (50 shorter events, 1.4 us)
Async XLA Ops:
  6.5 438.2 %copy-start = (bf16[1,1024,1024]{2,1,0:T(8,128)(2,1)S(1)}, bf16[1,1024,1024]{2,1,0:T(8,128)(2,1)}, u32[]{:S(2)}) copy-start(bf16[1,1024,1024]{2,1,0:T(8,128)(2,1)} %param.18) | copy-start | bytes 6291460
  11.2 16.7 %copy-start.1 = (bf16[1,192,1024]{2,1,0:T(8,128)(2,1)S(1)}, bf16[1,192,1024]{2,1,0:T(8,128)(2,1)}, u32[]{:S(2)}) copy-start(bf16[1,192,1024]{2,1,0:T(8,128)(2,1)} %param.11) | copy-start | bytes 1179652
  11.2 219.2 %all-to-all-start = ((bf16[64,128,384]{2,1,0:T(8,128)(2,1)}), bf16[64,128,384]{2,1,0:T(8,128)(2,1)}, u32[]{:S(2)}, u32[]{:S(2)}) async-start(bf16[64,128,384]{2,1,0:T(8,128)(2,1)} %tile.2), calls=%async_computation | async-start | bytes 12582912 | tf_op jit(solution)/shard_map/all_to_all | solution.py:15
  235.7 27.4 %copy-start.5 = (s32[1,192,2]{1,2,0:T(2,128)S(1)}, s32[1,192,2]{1,2,0:T(2,128)}, u32[]{:S(2)}) copy-start(s32[1,192,2]{1,2,0:T(2,128)} %param.16) | copy-start | bytes 4612
  235.7 27.8 %copy-start.6 = (s32[1,12,12]{2,0,1:T(1,128)S(1)}, s32[1,12,12]{2,0,1:T(1,128)}, u32[]{:S(2)}) copy-start(s32[1,12,12]{2,0,1:T(1,128)} %param.12) | copy-start | bytes 1732
  235.7 52.5 %all-to-all-start.1 = ((bf16[192,8,384]{2,0,1:T(8,128)(2,1)}), bf16[192,8,384]{2,0,1:T(8,128)(2,1)S(1)}, u32[]{:S(2)}, u32[]{:S(2)}) async-start(bf16[192,8,384]{2,0,1:T(8,128)(2,1)} %bitcast_convert_fusion), calls=%async_computation.1 | async-start | bytes 2359296 | tf_op jit(solution)/shard_map/all_to_all | solution.py:39
  262.3 98.1 %all-gather.3.cloned.1.call-start = ((), (), s32[]{:S(2)}) async-start(), calls=%async_computation.5 | async-start | bytes 2129920 | tf_op jit(solution)/shard_map/all_gather | solution.py:29
  295.7 3.5 copy-start.4
  305.0 3.5 copy-start.4
  314.3 3.5 copy-start.4
  325.5 38.9 %all-to-all-start.2 = ((bf16[8,192,128]{2,1,0:T(8,128)(2,1)}), bf16[8,192,128]{2,1,0:T(8,128)(2,1)S(1)}, u32[]{:S(2)}, u32[]{:S(2)}) async-start(bf16[8,192,128]{2,1,0:T(8,128)(2,1)} %reshape.146), calls=%async_computation.2 | async-start | bytes 786432 | tf_op jit(solution)/shard_map/all_to_all | solution.py:68
  360.4 4.7 copy-start.2
  364.4 3.4 copy-start.7
  364.4 0.7 copy-start.3
  444.7 3.3 copy-start.9
  453.8 9.1 %copy-start.8 = (f32[1,192,2]{1,2,0:T(2,128)S(1)}, f32[1,192,2]{1,2,0:T(2,128)}, u32[]{:S(2)}) copy-start(f32[1,192,2]{1,2,0:T(2,128)} %param.17) | copy-start | bytes 4612
  453.8 60.7 %all-to-all-start.4 = ((bf16[64,12,1024]{2,1,0:T(8,128)(2,1)}), bf16[64,12,1024]{2,1,0:T(8,128)(2,1)}, u32[]{:S(2)}, u32[]{:S(2)}) async-start(bf16[64,12,1024]{2,1,0:T(8,128)(2,1)} %reshape.121), calls=%async_computation.4 | async-start | bytes 4194304 | tf_op jit(solution)/shard_map/all_to_all | solution.py:99
Sparse Core Ops, SparseCore 0:
  266.2 94.1 all-gather.2
